TPU v7x, 256 devices: a whole 4x4x8 slice. The times are simulated.
256 devices in a mesh: seq: 128 (over x, y, z_lo, core), dp: 2 (over z_hi).
Axes of the slice: x: 4, y: 4, z: 8 (z_hi: 2, z_lo: 4; z = z_hi * 4 + z_lo), core: 2. Of those that a mesh axis runs over, the one named last changes fastest.
Arguments:
- inputs: bfloat16 [2, 256, 256, 512], P('dp', 'seq'), may hold values from -6 to 6
- gate: bfloat16 [2, 256, 256, 512], P('dp', 'seq'), may hold values from -6 to 6
- kernel: bfloat16 [256, 256, 512], P(None, 'seq'), may hold values from -6 to 6
- first_blocks: bfloat16 [256, 256, 256], P('seq'), may hold values from -0.375 to 0.375
- second_blocks: bfloat16 [256, 256, 256], P('seq'), may hold values from -0.375 to 0.375
- cotangent: bfloat16 [2, 256, 256, 512], P('dp', 'seq'), may hold values from -6 to 6
Outputs:
- mixed: bfloat16 [2, 256, 256, 512], P('dp', 'seq')
- grad_inputs: bfloat16 [2, 256, 256, 512], P('dp', 'seq')
- grad_gate: bfloat16 [2, 256, 256, 512], P('dp', 'seq')
- grad_kernel: float32 [256, 256, 512], P(None, 'seq')
All inputs are finite; a program needn't handle non-finite values.
Results may differ from a plain program's by a relative error of at most 0.007.
Values may be sent and summed in bfloat16 or wider, within the bound.
No kernel may reach another device: no remote copies, remote signals or barrier semaphores. Data moves between devices by JAX's collectives and lax.ppermute only.
A program may use at most 64 MiB of HBM per device.

v0:
```python
import jax
import jax.numpy as jnp
from jax import lax
from jax.sharding import PartitionSpec as P


def layer(inputs, gate, kernel, first_blocks, second_blocks, cotangent):
    f32 = jnp.float32
    bf16 = jnp.bfloat16
    n_seq = lax.axis_size("seq")
    n_dp = lax.axis_size("dp")
    col = lax.axis_index("dp")
    cols = second_blocks.shape[0]
    rows = first_blocks.shape[0]
    width = first_blocks.shape[1]
    dm = inputs.shape[-1]
    gate32 = gate[0].astype(f32)
    cot = cotangent[0].astype(f32)
    d_result = (cot * gate32).astype(bf16)

    blk1 = first_blocks.reshape(rows, n_seq, cols, width)
    blk1 = jnp.swapaxes(blk1, 1, 2).reshape(rows, n_seq * cols, width)
    blk2 = lax.dynamic_index_in_dim(second_blocks, col, axis=0, keepdims=False)
    kern = lax.dynamic_index_in_dim(kernel, col, axis=1, keepdims=False).astype(f32)

    both = jnp.concatenate([inputs[0], d_result], axis=-1)
    first = jnp.einsum("rij,rjf->irf", blk1, both, preferred_element_type=f32).astype(bf16)
    cols_in = lax.all_to_all(first, ("dp", "seq"), split_axis=0, concat_axis=0, tiled=True)
    cols_in = cols_in.reshape(n_dp, n_seq * rows, 2 * dm)
    mixed_both = jnp.einsum("qr,srf->sqf", blk2, cols_in, preferred_element_type=f32)
    second = mixed_both[..., :dm]
    d_hidden = mixed_both[..., dm:]
    own = jnp.sum(d_hidden * second, axis=0)
    pair = lax.all_gather(own, "dp", axis=1)
    kern2 = jnp.concatenate([kern, kern], axis=-1)
    scaled = (mixed_both * kern2).astype(bf16)
    unmixed = jnp.einsum("qr,sqf->srf", blk2, scaled, preferred_element_type=f32).astype(bf16)
    unmixed = unmixed.reshape(n_dp * n_seq, rows, 2 * dm)
    gathered = lax.all_to_all(unmixed, ("dp", "seq"), split_axis=0, concat_axis=0, tiled=True)
    out_both = jnp.einsum("rij,irf->rjf", blk1, gathered, preferred_element_type=f32)
    result = out_both[..., :dm]
    mixed = (result * gate32).astype(bf16)[None]
    grad_gate = (cot * result).astype(bf16)[None]
    grad_inputs = out_both[..., dm:].astype(bf16)[None]
    return (mixed, grad_inputs, grad_gate, pair)


def solution(mesh):
    placed = (
        P("dp", "seq", None, None),
        P("dp", "seq", None, None),
        P(None, "seq", None),
        P("seq", None, None),
        P("seq", None, None),
        P("dp", "seq", None, None),
    )
    return jax.shard_map(
        layer,
        mesh=mesh,
        in_specs=placed,
        out_specs=(
            P("dp", "seq", None, None),
            P("dp", "seq", None, None),
            P("dp", "seq", None, None),
            P(None, "seq", None),
        ),
        check_vma=False,
    )
```

profile of v0, /device:TPU:1, one launch (start us, length us, event | category | flops | bytes accessed | tf_op | source)
XLA Modules:
  0.0 139.6 jit_solution(11970094857709886080)
XLA Ops:
  7.2 0.0 copy-start
  7.2 0.0 copy-start.4
  7.2 1.2 reshape.27
  8.4 1.2 copy.36
  9.7 0.2 copy.35
  9.9 0.0 copy-start.1
  9.9 1.0 copy.34
  10.9 0.1 fusion.3
  11.0 1.5 %fusion = bf16[256,2,1024]{0,2,1:T(8,128)(2,1)S(1)} fusion(bf16[2,256,256]{2,1,0:T(8,128)(2,1)S(1)} %bitcast.43, bf16[2,256,512]{1,2,0:T(8,128)(2,1)S(1)} %fusion.3, bf16[2,256,512]{1,2,0:T(8,128)(2,1)} %bitcast.45), kind=kOutput, calls=%fused_computation.5 | convolution fusion | flops 271056896 | bytes 2359296 | tf_op jit(solution)/shard_map/rij,rjf->irf/dot_general | solution.py:27
  12.6 2.1 %copy.38 = bf16[256,2,1024]{2,1,0:T(2,128)(2,1)} copy(bf16[256,2,1024]{0,2,1:T(8,128)(2,1)S(1)} %fusion) | data formatting | bytes 2097152 | tf_op jit(solution)/shard_map/convert_element_type | solution.py:27
  14.7 15.6 %all-to-all-start = ((bf16[256,2,1024]{2,1,0:T(2,128)(2,1)}), bf16[256,2,1024]{2,1,0:T(2,128)(2,1)S(1)}, u32[]{:S(2)}, u32[]{:S(2)}) async-start(bf16[256,2,1024]{2,1,0:T(2,128)(2,1)} %copy.38), calls=%async_computation | async-start | bytes 2097152 | tf_op jit(solution)/shard_map/all_to_all | solution.py:28
  30.3 0.5 constant_dynamic-slice_fusion
  30.9 0.1 maximum_convert_fusion
  31.0 1.3 copy.41
  32.4 28.9 %all-to-all-done = bf16[256,2,1024]{2,1,0:T(2,128)(2,1)S(1)} async-done(((bf16[256,2,1024]{2,1,0:T(2,128)(2,1)}), bf16[256,2,1024]{2,1,0:T(2,128)(2,1)S(1)}, u32[]{:S(2)}, u32[]{:S(2)}) %all-to-all-start) | async-done | bytes 1048608 | tf_op jit(solution)/shard_map/all_to_all | solution.py:28
  61.2 1.2 reshape.29
  62.4 1.8 %convolution_bitcast_fusion.1 = f32[2,256,1024]{1,2,0:T(8,128)S(1)} fusion(bf16[2,256,1024]{2,1,0:T(8,128)(2,1)} %reshape.29, bf16[2,256,256]{2,1,0:T(8,128)(2,1)} %param.10, s32[]{:T(128)S(6)} %select_n.6), kind=kOutput, calls=%fused_computation.2 | convolution fusion | flops 268435456 | bytes 3276804 | tf_op jit(solution)/shard_map/qr,srf->sqf/dot_general | solution.py:30
  64.3 1.5 %fusion.1 = bf16[2,256,1024]{2,1,0:T(8,128)(2,1)} fusion(f32[2,256,1024]{1,2,0:T(8,128)S(1)} %convolution_bitcast_fusion.1, f32[256,1024]{0,1:T(8,128)S(1)} %copy-done.3, bf16[2,256,256]{2,1,0:T(8,128)(2,1)S(1)} %copy-done.6, s32[]{:T(128)S(6)} %select_n.6), kind=kOutput, calls=%fused_computation.6 | convolution fusion | flops 270008320 | bytes 4325380 | tf_op jit(solution)/shard_map/qr,sqf->srf/dot_general | solution.py:37
  65.8 2.3 %reshape.30 = bf16[256,2,1024]{2,1,0:T(2,128)(2,1)} reshape(bf16[2,256,1024]{2,1,0:T(8,128)(2,1)} %fusion.1) | data formatting | bytes 2097152 | tf_op jit(solution)/shard_map/reshape | solution.py:38
  68.1 7.5 %all-to-all-start.1 = ((bf16[256,2,1024]{2,1,0:T(2,128)(2,1)}), bf16[256,2,1024]{2,1,0:T(2,128)(2,1)}, u32[]{:S(2)}, u32[]{:S(2)}) async-start(bf16[256,2,1024]{2,1,0:T(2,128)(2,1)} %reshape.30), calls=%async_computation.1 | async-start | bytes 2097152 | tf_op jit(solution)/shard_map/all_to_all | solution.py:39
  75.6 0.0 all-gather.3.cloned.1.call-start
  75.6 0.9 fusion.5
  76.6 0.0 all-gather.3.cloned.1.call-update
  76.6 48.7 %all-gather.3.cloned.1.call-done = f32[256,1024]{0,1:T(8,128)} async-done(((f32[256,512]{0,1:T(8,128)}), f32[256,1024]{0,1:T(8,128)}) %all-gather.3.cloned.1.call-update) | async-done | bytes 1048592 | tf_op jit(solution)/shard_map/all_gather | solution.py:34
  125.3 2.2 %copy.48 = f32[256,2,512]{2,1,0:T(2,128)} copy(f32[256,2,512]{0,2,1:T(8,128)} %bitcast.41) | data formatting | bytes 2097152
  127.6 0.0 all-to-all-done.1
  127.6 1.8 %convolution_bitcast_fusion = f32[2,256,1024]{1,2,0:T(8,128)S(1)} fusion(bf16[2,256,256]{2,1,0:T(8,128)(2,1)S(1)} %bitcast.44, bf16[256,2,1024]{2,1,0:T(2,128)(2,1)} %all-to-all-done.1), kind=kOutput, calls=%fused_computation.1 | convolution fusion | flops 268435456 | bytes 3407872 | tf_op jit(solution)/shard_map/rij,irf->rjf/dot_general | solution.py:40
  129.4 0.2 fusion.13
  129.7 0.1 fusion.11
  129.7 1.0 copy.46
  130.7 1.0 copy.47
  131.7 1.0 copy.45
  (13 shorter events, 0.1 us)
Async XLA Ops:
  7.2 23.2 %copy-start = (bf16[256,2,512]{2,1,0:T(2,128)(2,1)S(1)}, bf16[256,2,512]{2,1,0:T(2,128)(2,1)}, u32[]{:S(2)}) copy-start(bf16[256,2,512]{2,1,0:T(2,128)(2,1)} %param.8) | copy-start | bytes 1572868
  7.2 2.5 %copy-start.4 = (bf16[1,2,256,512]{3,2,1,0:T(8,128)(2,1)S(1)}, bf16[1,2,256,512]{3,2,1,0:T(8,128)(2,1)}, u32[]{:S(2)}) copy-start(bf16[1,2,256,512]{3,2,1,0:T(8,128)(2,1)} %param.11) | copy-start | bytes 1572868
  7.2 2.7 %copy-start.5 = (bf16[1,2,256,512]{3,2,1,0:T(8,128)(2,1)S(1)}, bf16[1,2,256,512]{3,2,1,0:T(8,128)(2,1)}, u32[]{:S(2)}) copy-start(bf16[1,2,256,512]{3,2,1,0:T(8,128)(2,1)} %param.6) | copy-start | bytes 1572868
  9.9 2.7 %copy-start.1 = (bf16[1,2,256,512]{2,3,1,0:T(8,128)(2,1)}, bf16[1,2,256,512]{2,3,1,0:T(8,128)(2,1)S(1)}, u32[]{:S(2)}) copy-start(bf16[1,2,256,512]{2,3,1,0:T(8,128)(2,1)S(1)} %copy.35) | copy-start | bytes 1572868
  14.7 46.6 %all-to-all-start = ((bf16[256,2,1024]{2,1,0:T(2,128)(2,1)}), bf16[256,2,1024]{2,1,0:T(2,128)(2,1)S(1)}, u32[]{:S(2)}, u32[]{:S(2)}) async-start(bf16[256,2,1024]{2,1,0:T(2,128)(2,1)} %copy.38), calls=%async_computation | async-start | bytes 2097152 | tf_op jit(solution)/shard_map/all_to_all | solution.py:28
  62.4 1.8 %copy-start.3 = (f32[256,1024]{0,1:T(8,128)S(1)}, f32[256,1024]{0,1:T(8,128)}, u32[]{:S(2)}) copy-start(f32[256,1024]{0,1:T(8,128)} %copy.41) | copy-start | bytes 3145732
  62.4 1.8 %copy-start.6 = (bf16[2,256,256]{2,1,0:T(8,128)(2,1)S(1)}, bf16[2,256,256]{2,1,0:T(8,128)(2,1)}, u32[]{:S(2)}) copy-start(bf16[2,256,256]{2,1,0:T(8,128)(2,1)} %param.10) | copy-start | bytes 786436
  68.1 59.5 %all-to-all-start.1 = ((bf16[256,2,1024]{2,1,0:T(2,128)(2,1)}), bf16[256,2,1024]{2,1,0:T(2,128)(2,1)}, u32[]{:S(2)}, u32[]{:S(2)}) async-start(bf16[256,2,1024]{2,1,0:T(2,128)(2,1)} %reshape.30), calls=%async_computation.1 | async-start | bytes 2097152 | tf_op jit(solution)/shard_map/all_to_all | solution.py:39
  75.6 49.7 %all-gather.3.cloned.1.call-start = ((), (), s32[]{:S(2)}) async-start(), calls=%async_computation.2 | async-start | bytes 1572864 | tf_op jit(solution)/shard_map/all_gather | solution.py:34
  127.6 1.8 %copy-start.2 = (bf16[1,2,256,512]{2,3,1,0:T(8,128)(2,1)S(1)}, bf16[1,2,256,512]{2,3,1,0:T(8,128)(2,1)}, u32[]{:S(2)}) copy-start(bf16[1,2,256,512]{2,3,1,0:T(8,128)(2,1)} %copy-done.1) | copy-start | bytes 1572868
Sparse Core Ops, SparseCore 0:
  78.8 46.4 all-gather.2
where the time goes:
time: 140 us
  waiting for transfers between devices  77.6 us (55%)
  starting transfers between devices  23.2 us (17%)
  local copies, waits for them, and re-layouts  16.5 us (12%)
  between operations  14.2 us (10%)
  matrix products  6.7 us (5%)
    all_gather x1, waiting for transfers between devices, layer(): pair = lax.all_gather(own, 'dp', axis=1)  48.7 us
    all_to_all x1, waiting for transfers between devices, layer(): lax.all_to_all(first, ('dp', 'seq'), split_axis=0, concat_axis=0, tiled=T...  28.9 us
    all_to_all x1, starting transfers between devices, layer(): lax.all_to_all(first, ('dp', 'seq'), split_axis=0, concat_axis=0, tiled=T...  15.6 us
    unnamed x22, local copies, waits for them, and re-layouts  7.78 us
    all_to_all x1, starting transfers between devices, layer(): lax.all_to_all(unmixed, ('dp', 'seq'), split_axis=0, concat_axis=0, tiled...  7.5 us
  transfers between devices with their start and end apart: 3, of which 2 were waited for; matrix products, arithmetic and copies ran while one was open for 4% of the time, Pallas kernels for 0%

commit v1 on v0

--- a/solution.py
+++ b/solution.py
@@ -1,6 +1,7 @@
 import jax
 import jax.numpy as jnp
 from jax import lax
+from jax.experimental.layout import Layout, with_layout_constraint
 from jax.sharding import PartitionSpec as P
 
 
@@ -24,24 +25,27 @@
     kern = lax.dynamic_index_in_dim(kernel, col, axis=1, keepdims=False).astype(f32)
 
     both = jnp.concatenate([inputs[0], d_result], axis=-1)
-    first = jnp.einsum("rij,rjf->irf", blk1, both, preferred_element_type=f32).astype(bf16)
-    cols_in = lax.all_to_all(first, ("dp", "seq"), split_axis=0, concat_axis=0, tiled=True)
-    cols_in = cols_in.reshape(n_dp, n_seq * rows, 2 * dm)
+    first = jnp.einsum("rij,rjf->irf", first_blocks, both, preferred_element_type=f32).astype(bf16)
+    cols_in = lax.all_to_all(first, ("seq", "dp"), split_axis=0, concat_axis=0, tiled=True)
+    cols_in = cols_in.reshape(n_seq, n_dp, rows, 2 * dm)
+    cols_in = jnp.swapaxes(cols_in, 0, 1).reshape(n_dp, n_seq * rows, 2 * dm)
     mixed_both = jnp.einsum("qr,srf->sqf", blk2, cols_in, preferred_element_type=f32)
     second = mixed_both[..., :dm]
     d_hidden = mixed_both[..., dm:]
     own = jnp.sum(d_hidden * second, axis=0)
-    pair = lax.all_gather(own, "dp", axis=1)
+    other = lax.ppermute(own, "dp", perm=[(0, 1), (1, 0)])
     kern2 = jnp.concatenate([kern, kern], axis=-1)
     scaled = (mixed_both * kern2).astype(bf16)
     unmixed = jnp.einsum("qr,sqf->srf", blk2, scaled, preferred_element_type=f32).astype(bf16)
     unmixed = unmixed.reshape(n_dp * n_seq, rows, 2 * dm)
     gathered = lax.all_to_all(unmixed, ("dp", "seq"), split_axis=0, concat_axis=0, tiled=True)
     out_both = jnp.einsum("rij,irf->rjf", blk1, gathered, preferred_element_type=f32)
+    out_both = with_layout_constraint(out_both, Layout((0, 1, 2)))
     result = out_both[..., :dm]
     mixed = (result * gate32).astype(bf16)[None]
     grad_gate = (cot * result).astype(bf16)[None]
     grad_inputs = out_both[..., dm:].astype(bf16)[None]
+    pair = jnp.where(col == 0, jnp.stack([own, other], axis=1), jnp.stack([other, own], axis=1))
     return (mixed, grad_inputs, grad_gate, pair)
 
 

time: 140 us -> 123 us (0.88)
  between operations: 14.2 us -> 0.8 us
  starting transfers between devices: 23.2 us -> 29.2 us
  waiting for transfers between devices: 77.6 us -> 72.3 us
  local copies, waits for them, and re-layouts: 16.5 us -> 11.4 us
  other arithmetic: 1.4 us -> 3 us
    all_gather x1 -> x0, waiting for transfers between devices: 48.7 us -> none  [layer(): pair = lax.all_gather(own, 'dp', axis=1)]
    ppermute x0 -> x1, waiting for transfers between devices: none -> 41.9 us  [layer(): other = lax.ppermute(own, 'dp', perm=[(0, 1), (1, 0)])]
    ppermute x0 -> x1, starting transfers between devices: none -> 6.42 us  [layer(): other = lax.ppermute(own, 'dp', perm=[(0, 1), (1, 0)])]
    unnamed x22 -> x14, local copies, waits for them, and re-layouts: 7.78 us -> 2.55 us
    all_to_all x1, waiting for transfers between devices: 28.9 us -> 30.4 us  [layer(): lax.all_to_all(first, ('seq', 'dp'), split_axis=0, concat_axis=0, tiled=T...]
where the time goes in v1:
time: 123 us; the launch traced here: 122 us
  waiting for transfers between devices  72.3 us (59%)
  starting transfers between devices  29.2 us (24%)
  local copies, waits for them, and re-layouts  11.4 us (9%)
  matrix products  5.53 us (4%)
  other arithmetic  3 us (2%)
    ppermute x1, waiting for transfers between devices, layer(): other = lax.ppermute(own, 'dp', perm=[(0, 1), (1, 0)])  41.9 us
    all_to_all x1, waiting for transfers between devices, layer(): lax.all_to_all(first, ('seq', 'dp'), split_axis=0, concat_axis=0, tiled=T...  30.4 us
    all_to_all x1, starting transfers between devices, layer(): lax.all_to_all(first, ('seq', 'dp'), split_axis=0, concat_axis=0, tiled=T...  15.6 us
    all_to_all x1, starting transfers between devices, layer(): lax.all_to_all(unmixed, ('dp', 'seq'), split_axis=0, concat_axis=0, tiled...  7.13 us
    ppermute x1, starting transfers between devices, layer(): other = lax.ppermute(own, 'dp', perm=[(0, 1), (1, 0)])  6.42 us
    unnamed x14, local copies, waits for them, and re-layouts  2.55 us
  transfers between devices with their start and end apart: 3, of which 2 were waited for; matrix products, arithmetic and copies ran while one was open for 4% of the time, Pallas kernels for 0%

profile of v1, /device:TPU:1, one launch (start us, length us, event | category | flops | bytes accessed | tf_op | source)
XLA Modules:
  0.0 122.3 jit_solution(6024865328018450335)
XLA Ops:
  0.6 0.0 copy-start
  0.6 1.4 %fusion.3 = bf16[2,256,512]{2,1,0:T(8,128)(2,1)S(1)} fusion(bf16[1,2,256,512]{3,2,1,0:T(8,128)(2,1)} %param.7, bf16[1,2,256,512]{3,2,1,0:T(8,128)(2,1)} %param.11), kind=kLoop, calls=%fused_computation.11 | loop fusion | flops 1048576 | bytes 1572864 | tf_op jit(solution)/shard_map/convert_element_type | solution.py:20
  2.0 1.7 %fusion = bf16[256,2,1024]{0,2,1:T(8,128)(2,1)S(1)} fusion(bf16[2,256,256]{2,1,0:T(8,128)(2,1)} %param.9, bf16[2,256,512]{2,1,0:T(8,128)(2,1)S(1)} %fusion.3, bf16[2,256,512]{2,1,0:T(8,128)(2,1)} %bitcast.51), kind=kOutput, calls=%fused_computation.5 | convolution fusion | flops 271056896 | bytes 2359296 | tf_op jit(solution)/shard_map/rij,rjf->irf/dot_general | solution.py:28
  3.7 2.1 %copy.28 = bf16[256,2,1024]{2,1,0:T(2,128)(2,1)} copy(bf16[256,2,1024]{0,2,1:T(8,128)(2,1)S(1)} %fusion) | data formatting | bytes 2097152 | tf_op jit(solution)/shard_map/convert_element_type | solution.py:28
  5.8 15.6 %all-to-all-start = ((bf16[256,2,1024]{2,1,0:T(2,128)(2,1)}), bf16[256,2,1024]{2,1,0:T(2,128)(2,1)S(1)}, u32[]{:S(2)}, u32[]{:S(2)}) async-start(bf16[256,2,1024]{2,1,0:T(2,128)(2,1)} %copy.28), calls=%async_computation | async-start | bytes 2097152 | tf_op jit(solution)/shard_map/all_to_all | solution.py:29
  21.5 0.5 constant_dynamic-slice_fusion
  22.1 0.1 maximum_convert_fusion
  22.2 0.0 copy-start.4
  22.2 1.3 %copy.32 = f32[256,1024]{0,1:T(8,128)} copy(f32[256,1024]{1,0:T(8,128)S(1)} %maximum_convert_fusion) | data formatting | bytes 2097152 | tf_op jit(solution)/shard_map/concatenate | solution.py:37
  23.5 30.4 %all-to-all-done = bf16[256,2,1024]{2,1,0:T(2,128)(2,1)S(1)} async-done(((bf16[256,2,1024]{2,1,0:T(2,128)(2,1)}), bf16[256,2,1024]{2,1,0:T(2,128)(2,1)S(1)}, u32[]{:S(2)}, u32[]{:S(2)}) %all-to-all-start) | async-done | bytes 1048608 | tf_op jit(solution)/shard_map/all_to_all | solution.py:29
  53.9 0.8 copy.29
  54.7 0.0 copy-start.1
  54.8 0.0 copy-done.4
  54.8 0.5 convolution_bitcast_fusion.1
  55.3 0.7 copy-done.1
  56.0 1.5 %fusion.1 = bf16[2,256,1024]{2,1,0:T(8,128)(2,1)} fusion(f32[2,256,1024]{1,2,0:T(8,128)S(1)} %convolution_bitcast_fusion.1, f32[256,1024]{0,1:T(8,128)S(1)} %copy-done.1, bf16[2,256,256]{2,1,0:T(8,128)(2,1)S(1)} %copy-done.4, s32[]{:T(128)S(6)} %select_n.14), kind=kOutput, calls=%fused_computation.6 | convolution fusion | flops 270008320 | bytes 4325380 | tf_op jit(solution)/shard_map/qr,sqf->srf/dot_general | solution.py:39
  57.5 2.3 %reshape.32 = bf16[256,2,1024]{2,1,0:T(2,128)(2,1)} reshape(bf16[2,256,1024]{2,1,0:T(8,128)(2,1)} %fusion.1) | data formatting | bytes 2097152 | tf_op jit(solution)/shard_map/reshape | solution.py:40
  59.8 7.1 %all-to-all-start.1 = ((bf16[256,2,1024]{2,1,0:T(2,128)(2,1)}), bf16[256,2,1024]{2,1,0:T(2,128)(2,1)}, u32[]{:S(2)}, u32[]{:S(2)}) async-start(bf16[256,2,1024]{2,1,0:T(2,128)(2,1)} %reshape.32), calls=%async_computation.1 | async-start | bytes 2097152 | tf_op jit(solution)/shard_map/all_to_all | solution.py:41
  66.9 0.1 fusion.5
  67.0 6.4 %collective-permute-start = (f32[256,512]{0,1:T(8,128)S(1)}, f32[256,512]{0,1:T(8,128)S(1)}, u32[]{:S(2)}, u32[]{:S(2)}) collective-permute-start(f32[256,512]{0,1:T(8,128)S(1)} %fusion.5), channel_id=1, source_target_pairs={{0,1},{1,0},{2,3},{3,2},{4,5},{5,4},{6,7},{7,6},{8,9},{9,8},{10,11... | collective-permute-start | bytes 1572872 | tf_op jit(solution)/shard_map/ppermute | solution.py:36
  73.5 0.1 reshape.33
  73.6 0.3 copy.35
  73.9 0.2 reshape.34
  74.1 0.2 copy.37
  74.3 41.9 %collective-permute-done = f32[256,512]{0,1:T(8,128)S(1)} collective-permute-done((f32[256,512]{0,1:T(8,128)S(1)}, f32[256,512]{0,1:T(8,128)S(1)}, u32[]{:S(2)}, u32[]{:S(2)}) %collective-permute-start) | collective-permute-done | bytes 524320 | tf_op jit(solution)/shard_map/ppermute | solution.py:36
  116.2 0.2 copy.38
  116.4 0.1 maximum_select_fusion
  116.5 1.8 %copy.39 = f32[256,2,512]{2,1,0:T(2,128)} copy(f32[256,2,512]{2,0,1:T(8,128)S(1)} %maximum_select_fusion) | data formatting | bytes 2097152
  118.3 0.0 all-to-all-done.1
  118.3 1.8 %convolution_bitcast_fusion = f32[2,256,1024]{2,1,0:T(8,128)S(1)} fusion(bf16[2,256,256]{1,2,0:T(8,128)(2,1)S(1)} %reshape.34, bf16[256,2,1024]{2,1,0:T(2,128)(2,1)} %all-to-all-done.1), kind=kOutput, calls=%fused_computation.1 | convolution fusion | flops 268435456 | bytes 3407872 | tf_op jit(solution)/shard_map/rij,irf->rjf/dot_general | solution.py:42
  120.1 0.9 fusion.12
  121.0 1.3 %fusion.14 = (bf16[1,2,256,512]{3,2,1,0:T(8,128)(2,1)}, bf16[1,2,256,512]{3,2,1,0:T(8,128)(2,1)}) fusion(f32[2,256,1024]{2,1,0:T(8,128)S(1)} %convolution_bitcast_fusion, bf16[1,2,256,512]{3,2,1,0:T(8,128)(2,1)S(1)} %copy-done.3, bf16[1,2,256,512]{3,2,1,0:T(8,128)(2,1)S(1)} %copy-done.2), kind=kLoop, calls=%fused_computation.25 | loop fusion | flops 1572864 | bytes 3145728 | tf_op jit(solution)/shard_map/broadcast_in_dim | solution.py:46
  (8 shorter events, 0.1 us)
Async XLA Ops:
  0.6 20.8 %copy-start = (bf16[256,2,512]{2,1,0:T(2,128)(2,1)S(1)}, bf16[256,2,512]{2,1,0:T(2,128)(2,1)}, u32[]{:S(2)}) copy-start(bf16[256,2,512]{2,1,0:T(2,128)(2,1)} %param.8) | copy-start | bytes 1572868
  5.8 48.1 %all-to-all-start = ((bf16[256,2,1024]{2,1,0:T(2,128)(2,1)}), bf16[256,2,1024]{2,1,0:T(2,128)(2,1)S(1)}, u32[]{:S(2)}, u32[]{:S(2)}) async-start(bf16[256,2,1024]{2,1,0:T(2,128)(2,1)} %copy.28), calls=%async_computation | async-start | bytes 2097152 | tf_op jit(solution)/shard_map/all_to_all | solution.py:29
  22.2 32.6 %copy-start.4 = (bf16[2,256,256]{2,1,0:T(8,128)(2,1)S(1)}, bf16[2,256,256]{2,1,0:T(8,128)(2,1)}, u32[]{:S(2)}) copy-start(bf16[2,256,256]{2,1,0:T(8,128)(2,1)} %param.10) | copy-start | bytes 786436
  54.7 1.2 %copy-start.1 = (f32[256,1024]{0,1:T(8,128)S(1)}, f32[256,1024]{0,1:T(8,128)}, u32[]{:S(2)}) copy-start(f32[256,1024]{0,1:T(8,128)} %copy.32) | copy-start | bytes 3145732
  59.8 13.7 %copy-start.5 = (bf16[2,256,256]{2,1,0:T(8,128)(2,1)S(1)}, bf16[2,256,256]{2,1,0:T(8,128)(2,1)}, u32[]{:S(2)}) copy-start(bf16[2,256,256]{2,1,0:T(8,128)(2,1)} %param.9) | copy-start | bytes 786436
  59.8 58.5 %all-to-all-start.1 = ((bf16[256,2,1024]{2,1,0:T(2,128)(2,1)}), bf16[256,2,1024]{2,1,0:T(2,128)(2,1)}, u32[]{:S(2)}, u32[]{:S(2)}) async-start(bf16[256,2,1024]{2,1,0:T(2,128)(2,1)} %reshape.32), calls=%async_computation.1 | async-start | bytes 2097152 | tf_op jit(solution)/shard_map/all_to_all | solution.py:41
  67.0 49.1 %collective-permute-start = (f32[256,512]{0,1:T(8,128)S(1)}, f32[256,512]{0,1:T(8,128)S(1)}, u32[]{:S(2)}, u32[]{:S(2)}) collective-permute-start(f32[256,512]{0,1:T(8,128)S(1)} %fusion.5), channel_id=1, source_target_pairs={{0,1},{1,0},{2,3},{3,2},{4,5},{5,4},{6,7},{7,6},{8,9},{9,8},{10,11... | collective-permute-start | bytes 1572872 | tf_op jit(solution)/shard_map/ppermute | solution.py:36
  118.3 2.7 %copy-start.2 = (bf16[1,2,256,512]{3,2,1,0:T(8,128)(2,1)S(1)}, bf16[1,2,256,512]{3,2,1,0:T(8,128)(2,1)}, u32[]{:S(2)}) copy-start(bf16[1,2,256,512]{3,2,1,0:T(8,128)(2,1)} %param.7) | copy-start | bytes 1572868
  118.3 2.7 %copy-start.3 = (bf16[1,2,256,512]{3,2,1,0:T(8,128)(2,1)S(1)}, bf16[1,2,256,512]{3,2,1,0:T(8,128)(2,1)}, u32[]{:S(2)}) copy-start(bf16[1,2,256,512]{3,2,1,0:T(8,128)(2,1)} %param.11) | copy-start | bytes 1572868

commit v2 on v1

--- a/solution.py
+++ b/solution.py
@@ -39,12 +39,14 @@
     unmixed = jnp.einsum("qr,sqf->srf", blk2, scaled, preferred_element_type=f32).astype(bf16)
     unmixed = unmixed.reshape(n_dp * n_seq, rows, 2 * dm)
     gathered = lax.all_to_all(unmixed, ("dp", "seq"), split_axis=0, concat_axis=0, tiled=True)
-    out_both = jnp.einsum("rij,irf->rjf", blk1, gathered, preferred_element_type=f32)
-    out_both = with_layout_constraint(out_both, Layout((0, 1, 2)))
-    result = out_both[..., :dm]
+    def finish(x):
+        y = jnp.einsum("rij,ird->rjd", blk1, x, preferred_element_type=f32)
+        return with_layout_constraint(y, Layout((0, 1, 2)))
+
+    result = finish(gathered[..., :dm])
     mixed = (result * gate32).astype(bf16)[None]
     grad_gate = (cot * result).astype(bf16)[None]
-    grad_inputs = out_both[..., dm:].astype(bf16)[None]
+    grad_inputs = finish(gathered[..., dm:]).astype(bf16)[None]
     pair = jnp.where(col == 0, jnp.stack([own, other], axis=1), jnp.stack([other, own], axis=1))
     return (mixed, grad_inputs, grad_gate, pair)
 

time: 123 us -> 123 us (level)
  other arithmetic: 3 us -> 1.73 us
    slice x0 -> x1, local copies, waits for them, and re-layouts: none -> 1.92 us  [layer(): grad_inputs = finish(gathered[..., dm:]).astype(bf16)[None]]
    broadcast_in_dim x1 -> x0, other arithmetic: 1.27 us -> none  [layer(): grad_gate = (cot * result).astype(bf16)[None]]
where the time goes in v2:
time: 123 us
  waiting for transfers between devices  72.3 us (59%)
  starting transfers between devices  29.2 us (24%)
  local copies, waits for them, and re-layouts  12.5 us (10%)
  matrix products  6.1 us (5%)
  other arithmetic  1.73 us (1%)
    ppermute x1, waiting for transfers between devices, layer(): other = lax.ppermute(own, 'dp', perm=[(0, 1), (1, 0)])  41.9 us
    all_to_all x1, waiting for transfers between devices, layer(): lax.all_to_all(first, ('seq', 'dp'), split_axis=0, concat_axis=0, tiled=T...  30.4 us
    all_to_all x1, starting transfers between devices, layer(): lax.all_to_all(first, ('seq', 'dp'), split_axis=0, concat_axis=0, tiled=T...  15.6 us
    all_to_all x1, starting transfers between devices, layer(): lax.all_to_all(unmixed, ('dp', 'seq'), split_axis=0, concat_axis=0, tiled...  7.14 us
    ppermute x1, starting transfers between devices, layer(): other = lax.ppermute(own, 'dp', perm=[(0, 1), (1, 0)])  6.42 us
    unnamed x14, local copies, waits for them, and re-layouts  2.56 us
  transfers between devices with their start and end apart: 3, of which 2 were waited for; matrix products, arithmetic and copies ran while one was open for 4% of the time, Pallas kernels for 0%

profile of v2, /device:TPU:1, one launch (start us, length us, event | category | flops | bytes accessed | tf_op | source)
XLA Modules:
  0.0 122.7 jit_solution(11649851560098366595)
XLA Ops:
  0.6 0.0 copy-start
  0.6 1.4 %fusion.5 = bf16[2,256,512]{2,1,0:T(8,128)(2,1)S(1)} fusion(bf16[1,2,256,512]{3,2,1,0:T(8,128)(2,1)} %param.7, bf16[1,2,256,512]{3,2,1,0:T(8,128)(2,1)} %param.11), kind=kLoop, calls=%fused_computation.14 | loop fusion | flops 1048576 | bytes 1572864 | tf_op jit(solution)/shard_map/convert_element_type | solution.py:20
  2.0 1.7 %fusion = bf16[256,2,1024]{0,2,1:T(8,128)(2,1)S(1)} fusion(bf16[2,256,256]{2,1,0:T(8,128)(2,1)} %param.9, bf16[2,256,512]{2,1,0:T(8,128)(2,1)S(1)} %fusion.5, bf16[2,256,512]{2,1,0:T(8,128)(2,1)} %bitcast.60), kind=kOutput, calls=%fused_computation.4 | convolution fusion | flops 271056896 | bytes 2359296 | tf_op jit(solution)/shard_map/rij,rjf->irf/dot_general | solution.py:28
  3.7 2.1 %copy.28 = bf16[256,2,1024]{2,1,0:T(2,128)(2,1)} copy(bf16[256,2,1024]{0,2,1:T(8,128)(2,1)S(1)} %fusion) | data formatting | bytes 2097152 | tf_op jit(solution)/shard_map/convert_element_type | solution.py:28
  5.8 15.6 %all-to-all-start = ((bf16[256,2,1024]{2,1,0:T(2,128)(2,1)}), bf16[256,2,1024]{2,1,0:T(2,128)(2,1)S(1)}, u32[]{:S(2)}, u32[]{:S(2)}) async-start(bf16[256,2,1024]{2,1,0:T(2,128)(2,1)} %copy.28), calls=%async_computation | async-start | bytes 2097152 | tf_op jit(solution)/shard_map/all_to_all | solution.py:29
  21.5 0.5 constant_dynamic-slice_fusion
  22.1 0.1 maximum_convert_fusion
  22.2 0.0 copy-start.4
  22.2 1.3 %copy.32 = f32[256,1024]{0,1:T(8,128)} copy(f32[256,1024]{1,0:T(8,128)S(1)} %maximum_convert_fusion) | data formatting | bytes 2097152 | tf_op jit(solution)/shard_map/concatenate | solution.py:37
  23.5 30.4 %all-to-all-done = bf16[256,2,1024]{2,1,0:T(2,128)(2,1)S(1)} async-done(((bf16[256,2,1024]{2,1,0:T(2,128)(2,1)}), bf16[256,2,1024]{2,1,0:T(2,128)(2,1)S(1)}, u32[]{:S(2)}, u32[]{:S(2)}) %all-to-all-start) | async-done | bytes 1048608 | tf_op jit(solution)/shard_map/all_to_all | solution.py:29
  53.9 0.8 copy.29
  54.8 0.5 convolution_bitcast_fusion
  55.3 0.7 copy-done.1
  56.0 1.5 %fusion.1 = bf16[2,256,1024]{2,1,0:T(8,128)(2,1)} fusion(f32[2,256,1024]{1,2,0:T(8,128)S(1)} %convolution_bitcast_fusion, f32[256,1024]{0,1:T(8,128)S(1)} %copy-done.1, bf16[2,256,256]{2,1,0:T(8,128)(2,1)S(1)} %copy-done.4, s32[]{:T(128)S(6)} %select_n.14), kind=kOutput, calls=%fused_computation.5 | convolution fusion | flops 270008320 | bytes 4325380 | tf_op jit(solution)/shard_map/qr,sqf->srf/dot_general | solution.py:39
  57.5 2.3 %reshape.32 = bf16[256,2,1024]{2,1,0:T(2,128)(2,1)} reshape(bf16[2,256,1024]{2,1,0:T(8,128)(2,1)} %fusion.1) | data formatting | bytes 2097152 | tf_op jit(solution)/shard_map/reshape | solution.py:40
  59.8 7.1 %all-to-all-start.1 = ((bf16[256,2,1024]{2,1,0:T(2,128)(2,1)}), bf16[256,2,1024]{2,1,0:T(2,128)(2,1)}, u32[]{:S(2)}, u32[]{:S(2)}) async-start(bf16[256,2,1024]{2,1,0:T(2,128)(2,1)} %reshape.32), calls=%async_computation.1 | async-start | bytes 2097152 | tf_op jit(solution)/shard_map/all_to_all | solution.py:41
  66.9 0.1 fusion.7
  67.1 6.4 %collective-permute-start = (f32[256,512]{0,1:T(8,128)S(1)}, f32[256,512]{0,1:T(8,128)S(1)}, u32[]{:S(2)}, u32[]{:S(2)}) collective-permute-start(f32[256,512]{0,1:T(8,128)S(1)} %fusion.7), channel_id=1, source_target_pairs={{0,1},{1,0},{2,3},{3,2},{4,5},{5,4},{6,7},{7,6},{8,9},{9,8},{10,11... | collective-permute-start | bytes 1572872 | tf_op jit(solution)/shard_map/ppermute | solution.py:36
  73.5 0.1 reshape.33
  73.6 0.3 copy.36
  73.9 0.2 reshape.34
  74.1 0.2 copy.38
  74.3 41.9 %collective-permute-done = f32[256,512]{0,1:T(8,128)S(1)} collective-permute-done((f32[256,512]{0,1:T(8,128)S(1)}, f32[256,512]{0,1:T(8,128)S(1)}, u32[]{:S(2)}, u32[]{:S(2)}) %collective-permute-start) | collective-permute-done | bytes 524320 | tf_op jit(solution)/shard_map/ppermute | solution.py:36
  116.2 0.2 copy.39
  116.4 0.1 maximum_select_fusion
  116.5 0.0 copy-start.2
  116.5 0.0 copy-start.3
  116.5 1.8 %copy.40 = f32[256,2,512]{2,1,0:T(2,128)} copy(f32[256,2,512]{2,0,1:T(8,128)S(1)} %maximum_select_fusion) | data formatting | bytes 2097152
  118.3 0.0 all-to-all-done.1
  118.3 1.9 %fusion.24 = (bf16[256,2,512]{2,1,0:T(2,128)(2,1)S(1)}, bf16[256,2,512]{2,1,0:T(2,128)(2,1)S(1)}) fusion(bf16[256,2,1024]{2,1,0:T(2,128)(2,1)} %all-to-all-done.1), kind=kLoop, calls=%fused_computation.38 | loop fusion | bytes 2097152 | tf_op jit(solution)/shard_map/slice | solution.py:49
  120.2 1.3 %fusion.14 = (bf16[1,2,256,512]{3,2,1,0:T(8,128)(2,1)}, bf16[1,2,256,512]{3,2,1,0:T(8,128)(2,1)}) fusion(bf16[1,2,256,512]{3,2,1,0:T(8,128)(2,1)S(1)} %copy-done.2, bf16[1,2,256,512]{3,2,1,0:T(8,128)(2,1)S(1)} %copy-done.3, bf16[2,256,256]{1,2,0:T(8,128)(2,1)S(1)} %reshape.34, bf16[256,2,512]{2,1,0:T(2,128)(2,1)S(1)} %get-tuple-element.15), kind=kOutput, calls=%fused_computation.25 | convolution fusion | flops 135790592 | bytes 2883584 | tf_op jit(solution)/shard_map/rij,ird->rjd/dot_general | solution.py:43
  121.6 1.1 fusion.3
  (8 shorter events, 0.1 us)
Async XLA Ops:
  0.6 20.8 %copy-start = (bf16[256,2,512]{2,1,0:T(2,128)(2,1)S(1)}, bf16[256,2,512]{2,1,0:T(2,128)(2,1)}, u32[]{:S(2)}) copy-start(bf16[256,2,512]{2,1,0:T(2,128)(2,1)} %param.8) | copy-start | bytes 1572868
  5.8 48.1 %all-to-all-start = ((bf16[256,2,1024]{2,1,0:T(2,128)(2,1)}), bf16[256,2,1024]{2,1,0:T(2,128)(2,1)S(1)}, u32[]{:S(2)}, u32[]{:S(2)}) async-start(bf16[256,2,1024]{2,1,0:T(2,128)(2,1)} %copy.28), calls=%async_computation | async-start | bytes 2097152 | tf_op jit(solution)/shard_map/all_to_all | solution.py:29
  22.2 32.6 %copy-start.4 = (bf16[2,256,256]{2,1,0:T(8,128)(2,1)S(1)}, bf16[2,256,256]{2,1,0:T(8,128)(2,1)}, u32[]{:S(2)}) copy-start(bf16[2,256,256]{2,1,0:T(8,128)(2,1)} %param.10) | copy-start | bytes 786436
  54.7 1.2 copy-start.1
  59.8 13.7 %copy-start.5 = (bf16[2,256,256]{2,1,0:T(8,128)(2,1)S(1)}, bf16[2,256,256]{2,1,0:T(8,128)(2,1)}, u32[]{:S(2)}) copy-start(bf16[2,256,256]{2,1,0:T(8,128)(2,1)} %param.9) | copy-start | bytes 786436
  59.8 58.5 %all-to-all-start.1 = ((bf16[256,2,1024]{2,1,0:T(2,128)(2,1)}), bf16[256,2,1024]{2,1,0:T(2,128)(2,1)}, u32[]{:S(2)}, u32[]{:S(2)}) async-start(bf16[256,2,1024]{2,1,0:T(2,128)(2,1)} %reshape.32), calls=%async_computation.1 | async-start | bytes 2097152 | tf_op jit(solution)/shard_map/all_to_all | solution.py:41
  67.1 49.1 %collective-permute-start = (f32[256,512]{0,1:T(8,128)S(1)}, f32[256,512]{0,1:T(8,128)S(1)}, u32[]{:S(2)}, u32[]{:S(2)}) collective-permute-start(f32[256,512]{0,1:T(8,128)S(1)} %fusion.7), channel_id=1, source_target_pairs={{0,1},{1,0},{2,3},{3,2},{4,5},{5,4},{6,7},{7,6},{8,9},{9,8},{10,11... | collective-permute-start | bytes 1572872 | tf_op jit(solution)/shard_map/ppermute | solution.py:36
  116.5 3.7 %copy-start.2 = (bf16[1,2,256,512]{3,2,1,0:T(8,128)(2,1)S(1)}, bf16[1,2,256,512]{3,2,1,0:T(8,128)(2,1)}, u32[]{:S(2)}) copy-start(bf16[1,2,256,512]{3,2,1,0:T(8,128)(2,1)} %param.11) | copy-start | bytes 1572868
  116.5 3.7 %copy-start.3 = (bf16[1,2,256,512]{3,2,1,0:T(8,128)(2,1)S(1)}, bf16[1,2,256,512]{3,2,1,0:T(8,128)(2,1)}, u32[]{:S(2)}) copy-start(bf16[1,2,256,512]{3,2,1,0:T(8,128)(2,1)} %param.7) | copy-start | bytes 1572868

commit v3 on v1

--- a/solution.py
+++ b/solution.py
@@ -28,8 +28,9 @@
     first = jnp.einsum("rij,rjf->irf", first_blocks, both, preferred_element_type=f32).astype(bf16)
     cols_in = lax.all_to_all(first, ("seq", "dp"), split_axis=0, concat_axis=0, tiled=True)
     cols_in = cols_in.reshape(n_seq, n_dp, rows, 2 * dm)
-    cols_in = jnp.swapaxes(cols_in, 0, 1).reshape(n_dp, n_seq * rows, 2 * dm)
-    mixed_both = jnp.einsum("qr,srf->sqf", blk2, cols_in, preferred_element_type=f32)
+    mixed_both = jnp.einsum(
+        "qkl,kslf->sqf", blk2.reshape(-1, n_seq, rows), cols_in, preferred_element_type=f32
+    )
     second = mixed_both[..., :dm]
     d_hidden = mixed_both[..., dm:]
     own = jnp.sum(d_hidden * second, axis=0)

time: 123 us -> 123 us (level)
  matrix products: 5.53 us -> 6.9 us
    dot_general x1, matrix products: 0.5 us -> 1.87 us  [layer(): jnp.einsum('qkl,kslf->sqf', blk2.reshape(-1, n_seq, rows), cols_in, prefe...]
    unnamed x14 -> x16, local copies, waits for them, and re-layouts: 2.55 us -> 2.82 us
where the time goes in v3:
time: 123 us
  waiting for transfers between devices  71.9 us (58%)
  starting transfers between devices  29.2 us (24%)
  local copies, waits for them, and re-layouts  11.2 us (9%)
  matrix products  6.9 us (6%)
  other arithmetic  3 us (2%)
    ppermute x1, waiting for transfers between devices, layer(): other = lax.ppermute(own, 'dp', perm=[(0, 1), (1, 0)])  41.9 us
    all_to_all x1, waiting for transfers between devices, layer(): lax.all_to_all(first, ('seq', 'dp'), split_axis=0, concat_axis=0, tiled=T...  30 us
    all_to_all x1, starting transfers between devices, layer(): lax.all_to_all(first, ('seq', 'dp'), split_axis=0, concat_axis=0, tiled=T...  15.6 us
    all_to_all x1, starting transfers between devices, layer(): lax.all_to_all(unmixed, ('dp', 'seq'), split_axis=0, concat_axis=0, tiled...  7.14 us
    ppermute x1, starting transfers between devices, layer(): other = lax.ppermute(own, 'dp', perm=[(0, 1), (1, 0)])  6.42 us
    unnamed x16, local copies, waits for them, and re-layouts  2.82 us
  transfers between devices with their start and end apart: 3, of which 2 were waited for; matrix products, arithmetic and copies ran while one was open for 4% of the time, Pallas kernels for 0%

profile of v3, /device:TPU:1, one launch (start us, length us, event | category | flops | bytes accessed | tf_op | source)
XLA Modules:
  0.0 123.1 jit_solution(1772249341497461070)
XLA Ops:
  0.6 0.0 copy-start
  0.6 1.4 %fusion.3 = bf16[2,256,512]{2,1,0:T(8,128)(2,1)S(1)} fusion(bf16[1,2,256,512]{3,2,1,0:T(8,128)(2,1)} %param.7, bf16[1,2,256,512]{3,2,1,0:T(8,128)(2,1)} %param.11), kind=kLoop, calls=%fused_computation.11 | loop fusion | flops 1048576 | bytes 1572864 | tf_op jit(solution)/shard_map/convert_element_type | solution.py:20
  2.0 1.7 %fusion = bf16[256,2,1024]{0,2,1:T(8,128)(2,1)S(1)} fusion(bf16[2,256,256]{2,1,0:T(8,128)(2,1)} %param.9, bf16[2,256,512]{2,1,0:T(8,128)(2,1)S(1)} %fusion.3, bf16[2,256,512]{2,1,0:T(8,128)(2,1)} %bitcast.52), kind=kOutput, calls=%fused_computation.5 | convolution fusion | flops 271056896 | bytes 2359296 | tf_op jit(solution)/shard_map/rij,rjf->irf/dot_general | solution.py:28
  3.7 0.0 copy-start.6
  3.7 2.1 %copy.29 = bf16[256,2,1024]{2,1,0:T(2,128)(2,1)} copy(bf16[256,2,1024]{0,2,1:T(8,128)(2,1)S(1)} %fusion) | data formatting | bytes 2097152 | tf_op jit(solution)/shard_map/convert_element_type | solution.py:28
  5.8 15.6 %all-to-all-start = ((bf16[256,2,1024]{2,1,0:T(2,128)(2,1)}), bf16[256,2,1024]{2,1,0:T(2,128)(2,1)S(1)}, u32[]{:S(2)}, u32[]{:S(2)}) async-start(bf16[256,2,1024]{2,1,0:T(2,128)(2,1)} %copy.29), calls=%async_computation | async-start | bytes 2097152 | tf_op jit(solution)/shard_map/all_to_all | solution.py:29
  21.5 0.1 copy.30
  21.6 0.1 reshape.32
  21.7 0.1 copy.32
  21.8 0.5 constant_dynamic-slice_fusion
  22.4 0.1 maximum_convert_fusion
  22.6 1.3 %copy.34 = f32[256,1024]{0,1:T(8,128)} copy(f32[256,1024]{1,0:T(8,128)S(1)} %maximum_convert_fusion) | data formatting | bytes 2097152 | tf_op jit(solution)/shard_map/concatenate | solution.py:38
  23.9 30.0 %all-to-all-done = bf16[256,2,1024]{2,1,0:T(2,128)(2,1)S(1)} async-done(((bf16[256,2,1024]{2,1,0:T(2,128)(2,1)}), bf16[256,2,1024]{2,1,0:T(2,128)(2,1)S(1)}, u32[]{:S(2)}, u32[]{:S(2)}) %all-to-all-start) | async-done | bytes 1048608 | tf_op jit(solution)/shard_map/all_to_all | solution.py:29
  53.9 1.0 copy-done.1
  54.9 1.9 %convolution_bitcast_fusion.1 = f32[2,256,1024]{1,2,0:T(8,128)S(1)} fusion(bf16[128,2,2,1024]{3,2,1,0:T(2,128)(2,1)} %bitcast.47, bf16[256,128,2]{1,0,2:T(8,128)(2,1)S(1)} %copy.32), kind=kOutput, calls=%fused_computation.2 | convolution fusion | flops 268435456 | bytes 3276800 | tf_op jit(solution)/shard_map/qkl,kslf->sqf/dot_general | solution.py:31
  56.8 1.5 %fusion.1 = bf16[2,256,1024]{2,1,0:T(8,128)(2,1)} fusion(f32[2,256,1024]{1,2,0:T(8,128)S(1)} %convolution_bitcast_fusion.1, f32[256,1024]{0,1:T(8,128)S(1)} %copy-done.2, bf16[1,256,256]{2,1,0:T(8,128)(2,1)S(1)} %constant_dynamic-slice_fusion.1), kind=kOutput, calls=%fused_computation.6 | convolution fusion | flops 270008320 | bytes 4325376 | tf_op jit(solution)/shard_map/qr,sqf->srf/dot_general | solution.py:40
  58.3 2.3 %reshape.33 = bf16[256,2,1024]{2,1,0:T(2,128)(2,1)} reshape(bf16[2,256,1024]{2,1,0:T(8,128)(2,1)} %fusion.1) | data formatting | bytes 2097152 | tf_op jit(solution)/shard_map/reshape | solution.py:41
  60.6 7.1 %all-to-all-start.1 = ((bf16[256,2,1024]{2,1,0:T(2,128)(2,1)}), bf16[256,2,1024]{2,1,0:T(2,128)(2,1)}, u32[]{:S(2)}, u32[]{:S(2)}) async-start(bf16[256,2,1024]{2,1,0:T(2,128)(2,1)} %reshape.33), calls=%async_computation.1 | async-start | bytes 2097152 | tf_op jit(solution)/shard_map/all_to_all | solution.py:42
  67.7 0.1 fusion.5
  67.9 6.4 %collective-permute-start = (f32[256,512]{0,1:T(8,128)S(1)}, f32[256,512]{0,1:T(8,128)S(1)}, u32[]{:S(2)}, u32[]{:S(2)}) collective-permute-start(f32[256,512]{0,1:T(8,128)S(1)} %fusion.5), channel_id=1, source_target_pairs={{0,1},{1,0},{2,3},{3,2},{4,5},{5,4},{6,7},{7,6},{8,9},{9,8},{10,11... | collective-permute-start | bytes 1572872 | tf_op jit(solution)/shard_map/ppermute | solution.py:37
  74.3 0.1 reshape.34
  74.4 0.3 copy.37
  74.7 0.2 reshape.35
  74.9 0.2 copy.39
  75.1 41.9 %collective-permute-done = f32[256,512]{0,1:T(8,128)S(1)} collective-permute-done((f32[256,512]{0,1:T(8,128)S(1)}, f32[256,512]{0,1:T(8,128)S(1)}, u32[]{:S(2)}, u32[]{:S(2)}) %collective-permute-start) | collective-permute-done | bytes 524320 | tf_op jit(solution)/shard_map/ppermute | solution.py:37
  117.0 0.2 copy.40
  117.2 0.1 maximum_select_fusion
  117.3 1.8 %copy.41 = f32[256,2,512]{2,1,0:T(2,128)} copy(f32[256,2,512]{2,0,1:T(8,128)S(1)} %maximum_select_fusion) | data formatting | bytes 2097152
  119.1 0.0 all-to-all-done.1
  119.1 1.8 %convolution_bitcast_fusion = f32[2,256,1024]{2,1,0:T(8,128)S(1)} fusion(bf16[2,256,256]{1,2,0:T(8,128)(2,1)S(1)} %reshape.35, bf16[256,2,1024]{2,1,0:T(2,128)(2,1)} %all-to-all-done.1), kind=kOutput, calls=%fused_computation.1 | convolution fusion | flops 268435456 | bytes 3407872 | tf_op jit(solution)/shard_map/rij,irf->rjf/dot_general | solution.py:43
  120.9 0.9 fusion.12
  121.8 1.3 %fusion.14 = (bf16[1,2,256,512]{3,2,1,0:T(8,128)(2,1)}, bf16[1,2,256,512]{3,2,1,0:T(8,128)(2,1)}) fusion(f32[2,256,1024]{2,1,0:T(8,128)S(1)} %convolution_bitcast_fusion, bf16[1,2,256,512]{3,2,1,0:T(8,128)(2,1)S(1)} %copy-done.4, bf16[1,2,256,512]{3,2,1,0:T(8,128)(2,1)S(1)} %copy-done.3), kind=kLoop, calls=%fused_computation.25 | loop fusion | flops 1572864 | bytes 3145728 | tf_op jit(solution)/shard_map/broadcast_in_dim | solution.py:47
  (13 shorter events, 0.1 us)
Async XLA Ops:
  0.6 21.2 %copy-start = (bf16[256,2,512]{2,1,0:T(2,128)(2,1)S(1)}, bf16[256,2,512]{2,1,0:T(2,128)(2,1)}, u32[]{:S(2)}) copy-start(bf16[256,2,512]{2,1,0:T(2,128)(2,1)} %param.8) | copy-start | bytes 1572868
  3.7 17.8 %copy-start.6 = (bf16[2,256,256]{2,1,0:T(8,128)(2,1)S(1)}, bf16[2,256,256]{2,1,0:T(8,128)(2,1)}, u32[]{:S(2)}) copy-start(bf16[2,256,256]{2,1,0:T(8,128)(2,1)} %param.10) | copy-start | bytes 786436
  5.8 48.1 %all-to-all-start = ((bf16[256,2,1024]{2,1,0:T(2,128)(2,1)}), bf16[256,2,1024]{2,1,0:T(2,128)(2,1)S(1)}, u32[]{:S(2)}, u32[]{:S(2)}) async-start(bf16[256,2,1024]{2,1,0:T(2,128)(2,1)} %copy.29), calls=%async_computation | async-start | bytes 2097152 | tf_op jit(solution)/shard_map/all_to_all | solution.py:29
  53.9 1.0 copy-start.1
  54.9 1.9 %copy-start.2 = (f32[256,1024]{0,1:T(8,128)S(1)}, f32[256,1024]{0,1:T(8,128)}, u32[]{:S(2)}) copy-start(f32[256,1024]{0,1:T(8,128)} %copy.34) | copy-start | bytes 3145732
  60.6 13.7 %copy-start.5 = (bf16[2,256,256]{2,1,0:T(8,128)(2,1)S(1)}, bf16[2,256,256]{2,1,0:T(8,128)(2,1)}, u32[]{:S(2)}) copy-start(bf16[2,256,256]{2,1,0:T(8,128)(2,1)} %param.9) | copy-start | bytes 786436
  60.6 58.5 %all-to-all-start.1 = ((bf16[256,2,1024]{2,1,0:T(2,128)(2,1)}), bf16[256,2,1024]{2,1,0:T(2,128)(2,1)}, u32[]{:S(2)}, u32[]{:S(2)}) async-start(bf16[256,2,1024]{2,1,0:T(2,128)(2,1)} %reshape.33), calls=%async_computation.1 | async-start | bytes 2097152 | tf_op jit(solution)/shard_map/all_to_all | solution.py:42
  67.9 49.1 %collective-permute-start = (f32[256,512]{0,1:T(8,128)S(1)}, f32[256,512]{0,1:T(8,128)S(1)}, u32[]{:S(2)}, u32[]{:S(2)}) collective-permute-start(f32[256,512]{0,1:T(8,128)S(1)} %fusion.5), channel_id=1, source_target_pairs={{0,1},{1,0},{2,3},{3,2},{4,5},{5,4},{6,7},{7,6},{8,9},{9,8},{10,11... | collective-permute-start | bytes 1572872 | tf_op jit(solution)/shard_map/ppermute | solution.py:37
  119.1 2.7 %copy-start.3 = (bf16[1,2,256,512]{3,2,1,0:T(8,128)(2,1)S(1)}, bf16[1,2,256,512]{3,2,1,0:T(8,128)(2,1)}, u32[]{:S(2)}) copy-start(bf16[1,2,256,512]{3,2,1,0:T(8,128)(2,1)} %param.7) | copy-start | bytes 1572868
  119.1 2.7 %copy-start.4 = (bf16[1,2,256,512]{3,2,1,0:T(8,128)(2,1)S(1)}, bf16[1,2,256,512]{3,2,1,0:T(8,128)(2,1)}, u32[]{:S(2)}) copy-start(bf16[1,2,256,512]{3,2,1,0:T(8,128)(2,1)} %param.11) | copy-start | bytes 1572868

commit v4 on v3

--- a/solution.py
+++ b/solution.py
@@ -37,10 +37,12 @@
     other = lax.ppermute(own, "dp", perm=[(0, 1), (1, 0)])
     kern2 = jnp.concatenate([kern, kern], axis=-1)
     scaled = (mixed_both * kern2).astype(bf16)
-    unmixed = jnp.einsum("qr,sqf->srf", blk2, scaled, preferred_element_type=f32).astype(bf16)
-    unmixed = unmixed.reshape(n_dp * n_seq, rows, 2 * dm)
-    gathered = lax.all_to_all(unmixed, ("dp", "seq"), split_axis=0, concat_axis=0, tiled=True)
-    out_both = jnp.einsum("rij,irf->rjf", blk1, gathered, preferred_element_type=f32)
+    unmixed = jnp.einsum(
+        "qkl,sqf->kslf", blk2.reshape(-1, n_seq, rows), scaled, preferred_element_type=f32
+    ).astype(bf16)
+    unmixed = unmixed.reshape(n_seq * n_dp, rows, 2 * dm)
+    gathered = lax.all_to_all(unmixed, ("seq", "dp"), split_axis=0, concat_axis=0, tiled=True)
+    out_both = jnp.einsum("rij,irf->rjf", first_blocks, gathered, preferred_element_type=f32)
     out_both = with_layout_constraint(out_both, Layout((0, 1, 2)))
     result = out_both[..., :dm]
     mixed = (result * gate32).astype(bf16)[None]

time: 123 us -> 122 us (level)
    reshape x3 -> x0, local copies, waits for them, and re-layouts: 2.53 us -> none  [the longest x1 2.26 us: layer(): unmixed = unmixed.reshape(n_dp * n_seq, rows, 2 * dm)]
    convert_element_type x0 -> x1, local copies, waits for them, and re-layouts: none -> 2.1 us  [layer(): unmixed = jnp.einsum('qkl,sqf->kslf', blk2.reshape(-1, n_seq, rows), scal...]
where the time goes in v4:
time: 122 us
  waiting for transfers between devices  72.5 us (59%)
  starting transfers between devices  29.1 us (24%)
  local copies, waits for them, and re-layouts  10.5 us (9%)
  matrix products  5.92 us (5%)
  other arithmetic  3 us (2%)
    ppermute x1, waiting for transfers between devices, layer(): other = lax.ppermute(own, 'dp', perm=[(0, 1), (1, 0)])  42.5 us
    all_to_all x1, waiting for transfers between devices, layer(): lax.all_to_all(first, ('seq', 'dp'), split_axis=0, concat_axis=0, tiled=T...  30 us
    all_to_all x1, starting transfers between devices, layer(): lax.all_to_all(first, ('seq', 'dp'), split_axis=0, concat_axis=0, tiled=T...  15.6 us
    all_to_all x1, starting transfers between devices, layer(): lax.all_to_all(unmixed, ('seq', 'dp'), split_axis=0, concat_axis=0, tiled...  7.01 us
    ppermute x1, starting transfers between devices, layer(): other = lax.ppermute(own, 'dp', perm=[(0, 1), (1, 0)])  6.42 us
    unnamed x16, local copies, waits for them, and re-layouts  2.82 us
  transfers between devices with their start and end apart: 3, of which 2 were waited for; matrix products, arithmetic and copies ran while one was open for 4% of the time, Pallas kernels for 0%

profile of v4, /device:TPU:1, one launch (start us, length us, event | category | flops | bytes accessed | tf_op | source)
XLA Modules:
  0.0 121.8 jit_solution(7897307662074622520)
XLA Ops:
  0.6 0.0 copy-start
  0.6 1.4 %fusion.3 = bf16[2,256,512]{2,1,0:T(8,128)(2,1)S(1)} fusion(bf16[1,2,256,512]{3,2,1,0:T(8,128)(2,1)} %param.7, bf16[1,2,256,512]{3,2,1,0:T(8,128)(2,1)} %param.11), kind=kLoop, calls=%fused_computation.11 | loop fusion | flops 1048576 | bytes 1572864 | tf_op jit(solution)/shard_map/convert_element_type | solution.py:20
  2.0 1.7 %fusion = bf16[256,2,1024]{0,2,1:T(8,128)(2,1)S(1)} fusion(bf16[2,256,256]{2,1,0:T(8,128)(2,1)} %param.9, bf16[2,256,512]{2,1,0:T(8,128)(2,1)S(1)} %fusion.3, bf16[2,256,512]{2,1,0:T(8,128)(2,1)} %bitcast.53), kind=kOutput, calls=%fused_computation.5 | convolution fusion | flops 271056896 | bytes 2359296 | tf_op jit(solution)/shard_map/rij,rjf->irf/dot_general | solution.py:28
  3.7 0.0 copy-start.6
  3.7 2.1 %copy.29 = bf16[256,2,1024]{2,1,0:T(2,128)(2,1)} copy(bf16[256,2,1024]{0,2,1:T(8,128)(2,1)S(1)} %fusion) | data formatting | bytes 2097152 | tf_op jit(solution)/shard_map/convert_element_type | solution.py:28
  5.8 15.6 %all-to-all-start = ((bf16[256,2,1024]{2,1,0:T(2,128)(2,1)}), bf16[256,2,1024]{2,1,0:T(2,128)(2,1)S(1)}, u32[]{:S(2)}, u32[]{:S(2)}) async-start(bf16[256,2,1024]{2,1,0:T(2,128)(2,1)} %copy.29), calls=%async_computation | async-start | bytes 2097152 | tf_op jit(solution)/shard_map/all_to_all | solution.py:29
  21.5 0.0 copy-done.6
  21.5 0.1 copy.30
  21.6 0.1 reshape.27
  21.7 0.1 copy.32
  21.8 0.5 constant_dynamic-slice_fusion
  22.4 0.1 maximum_convert_fusion
  22.6 1.3 %copy.34 = f32[256,1024]{0,1:T(8,128)} copy(f32[256,1024]{1,0:T(8,128)S(1)} %maximum_convert_fusion) | data formatting | bytes 2097152 | tf_op jit(solution)/shard_map/concatenate | solution.py:38
  23.9 30.0 %all-to-all-done = bf16[256,2,1024]{2,1,0:T(2,128)(2,1)S(1)} async-done(((bf16[256,2,1024]{2,1,0:T(2,128)(2,1)}), bf16[256,2,1024]{2,1,0:T(2,128)(2,1)S(1)}, u32[]{:S(2)}, u32[]{:S(2)}) %all-to-all-start) | async-done | bytes 1048608 | tf_op jit(solution)/shard_map/all_to_all | solution.py:29
  53.9 1.0 copy-done.2
  54.9 1.9 %convolution_bitcast_fusion.1 = f32[2,256,1024]{1,2,0:T(8,128)S(1)} fusion(bf16[128,2,2,1024]{3,2,1,0:T(2,128)(2,1)} %bitcast.48, bf16[256,128,2]{1,0,2:T(8,128)(2,1)S(1)} %copy.32), kind=kOutput, calls=%fused_computation.2 | convolution fusion | flops 268435456 | bytes 3276800 | tf_op jit(solution)/shard_map/qkl,kslf->sqf/dot_general | solution.py:31
  56.8 0.5 fusion.1
  57.3 2.1 %copy.37 = bf16[128,2,2,1024]{3,2,1,0:T(2,128)(2,1)} copy(bf16[128,2,2,1024]{3,0,2,1:T(8,128)(2,1)S(1)} %fusion.1) | data formatting | bytes 2097152 | tf_op jit(solution)/shard_map/convert_element_type | solution.py:42
  59.4 7.0 %all-to-all-start.1 = ((bf16[256,2,1024]{2,1,0:T(2,128)(2,1)}), bf16[256,2,1024]{2,1,0:T(2,128)(2,1)}, u32[]{:S(2)}, u32[]{:S(2)}) async-start(bf16[256,2,1024]{2,1,0:T(2,128)(2,1)} %bitcast.49), calls=%async_computation.1 | async-start | bytes 2097152 | tf_op jit(solution)/shard_map/all_to_all | solution.py:44
  66.4 0.1 fusion.7
  66.6 6.4 %collective-permute-start = (f32[256,512]{0,1:T(8,128)S(1)}, f32[256,512]{0,1:T(8,128)S(1)}, u32[]{:S(2)}, u32[]{:S(2)}) collective-permute-start(f32[256,512]{0,1:T(8,128)S(1)} %fusion.7), channel_id=1, source_target_pairs={{0,1},{1,0},{2,3},{3,2},{4,5},{5,4},{6,7},{7,6},{8,9},{9,8},{10,11... | collective-permute-start | bytes 1572872 | tf_op jit(solution)/shard_map/ppermute | solution.py:37
  73.0 0.2 copy.40
  73.2 42.5 %collective-permute-done = f32[256,512]{0,1:T(8,128)S(1)} collective-permute-done((f32[256,512]{0,1:T(8,128)S(1)}, f32[256,512]{0,1:T(8,128)S(1)}, u32[]{:S(2)}, u32[]{:S(2)}) %collective-permute-start) | collective-permute-done | bytes 524320 | tf_op jit(solution)/shard_map/ppermute | solution.py:37
  115.7 0.2 copy.41
  115.9 0.0 copy-start.5
  115.9 0.1 maximum_select_fusion
  116.0 1.8 %copy.42 = f32[256,2,512]{2,1,0:T(2,128)} copy(f32[256,2,512]{2,0,1:T(8,128)S(1)} %maximum_select_fusion) | data formatting | bytes 2097152
  117.8 0.0 all-to-all-done.1
  117.8 1.9 %convolution_bitcast_fusion = f32[2,256,1024]{2,1,0:T(8,128)S(1)} fusion(bf16[2,256,256]{2,1,0:T(8,128)(2,1)S(1)} %copy-done.5, bf16[256,2,1024]{2,1,0:T(2,128)(2,1)} %all-to-all-done.1), kind=kOutput, calls=%fused_computation.1 | convolution fusion | flops 268435456 | bytes 3407872 | tf_op jit(solution)/shard_map/rij,irf->rjf/dot_general | solution.py:45
  119.6 0.9 fusion.14
  120.5 0.0 copy-done.3
  120.5 1.3 %fusion.16 = (bf16[1,2,256,512]{3,2,1,0:T(8,128)(2,1)}, bf16[1,2,256,512]{3,2,1,0:T(8,128)(2,1)}) fusion(f32[2,256,1024]{2,1,0:T(8,128)S(1)} %convolution_bitcast_fusion, bf16[1,2,256,512]{3,2,1,0:T(8,128)(2,1)S(1)} %copy-done.4, bf16[1,2,256,512]{3,2,1,0:T(8,128)(2,1)S(1)} %copy-done.3), kind=kLoop, calls=%fused_computation.26 | loop fusion | flops 1572864 | bytes 3145728 | tf_op jit(solution)/shard_map/broadcast_in_dim | solution.py:49
  (10 shorter events, 0.1 us)
Async XLA Ops:
  0.6 21.2 %copy-start = (bf16[256,2,512]{2,1,0:T(2,128)(2,1)S(1)}, bf16[256,2,512]{2,1,0:T(2,128)(2,1)}, u32[]{:S(2)}) copy-start(bf16[256,2,512]{2,1,0:T(2,128)(2,1)} %param.8) | copy-start | bytes 1572868
  3.7 17.8 %copy-start.6 = (bf16[2,256,256]{2,1,0:T(8,128)(2,1)S(1)}, bf16[2,256,256]{2,1,0:T(8,128)(2,1)}, u32[]{:S(2)}) copy-start(bf16[2,256,256]{2,1,0:T(8,128)(2,1)} %param.10) | copy-start | bytes 786436
  5.8 48.1 %all-to-all-start = ((bf16[256,2,1024]{2,1,0:T(2,128)(2,1)}), bf16[256,2,1024]{2,1,0:T(2,128)(2,1)S(1)}, u32[]{:S(2)}, u32[]{:S(2)}) async-start(bf16[256,2,1024]{2,1,0:T(2,128)(2,1)} %copy.29), calls=%async_computation | async-start | bytes 2097152 | tf_op jit(solution)/shard_map/all_to_all | solution.py:29
  53.9 1.0 copy-start.2
  54.9 1.9 %copy-start.1 = (f32[256,1024]{0,1:T(8,128)S(1)}, f32[256,1024]{0,1:T(8,128)}, u32[]{:S(2)}) copy-start(f32[256,1024]{0,1:T(8,128)} %copy.34) | copy-start | bytes 3145732
  59.4 58.4 %all-to-all-start.1 = ((bf16[256,2,1024]{2,1,0:T(2,128)(2,1)}), bf16[256,2,1024]{2,1,0:T(2,128)(2,1)}, u32[]{:S(2)}, u32[]{:S(2)}) async-start(bf16[256,2,1024]{2,1,0:T(2,128)(2,1)} %bitcast.49), calls=%async_computation.1 | async-start | bytes 2097152 | tf_op jit(solution)/shard_map/all_to_all | solution.py:44
  66.6 49.1 %collective-permute-start = (f32[256,512]{0,1:T(8,128)S(1)}, f32[256,512]{0,1:T(8,128)S(1)}, u32[]{:S(2)}, u32[]{:S(2)}) collective-permute-start(f32[256,512]{0,1:T(8,128)S(1)} %fusion.7), channel_id=1, source_target_pairs={{0,1},{1,0},{2,3},{3,2},{4,5},{5,4},{6,7},{7,6},{8,9},{9,8},{10,11... | collective-permute-start | bytes 1572872 | tf_op jit(solution)/shard_map/ppermute | solution.py:37
  115.9 1.9 %copy-start.5 = (bf16[2,256,256]{2,1,0:T(8,128)(2,1)S(1)}, bf16[2,256,256]{2,1,0:T(8,128)(2,1)}, u32[]{:S(2)}) copy-start(bf16[2,256,256]{2,1,0:T(8,128)(2,1)} %param.9) | copy-start | bytes 786436
  117.8 2.7 %copy-start.3 = (bf16[1,2,256,512]{3,2,1,0:T(8,128)(2,1)S(1)}, bf16[1,2,256,512]{3,2,1,0:T(8,128)(2,1)}, u32[]{:S(2)}) copy-start(bf16[1,2,256,512]{3,2,1,0:T(8,128)(2,1)} %param.7) | copy-start | bytes 1572868
  117.8 2.7 %copy-start.4 = (bf16[1,2,256,512]{3,2,1,0:T(8,128)(2,1)S(1)}, bf16[1,2,256,512]{3,2,1,0:T(8,128)(2,1)}, u32[]{:S(2)}) copy-start(bf16[1,2,256,512]{3,2,1,0:T(8,128)(2,1)} %param.11) | copy-start | bytes 1572868

commit v5 on v3

--- a/solution.py
+++ b/solution.py
@@ -34,7 +34,10 @@
     second = mixed_both[..., :dm]
     d_hidden = mixed_both[..., dm:]
     own = jnp.sum(d_hidden * second, axis=0)
-    other = lax.ppermute(own, "dp", perm=[(0, 1), (1, 0)])
+    half = own.shape[0] // 2
+    other_a = lax.ppermute(own[:half], "dp", perm=[(0, 1), (1, 0)])
+    other_b = lax.ppermute(own[half:], "dp", perm=[(0, 1), (1, 0)])
+    other = jnp.concatenate([other_a, other_b], axis=0)
     kern2 = jnp.concatenate([kern, kern], axis=-1)
     scaled = (mixed_both * kern2).astype(bf16)
     unmixed = jnp.einsum("qr,sqf->srf", blk2, scaled, preferred_element_type=f32).astype(bf16)

time: 123 us -> 123 us (level)
    ppermute x1 -> x2, waiting for transfers between devices: 41.9 us -> 41.7 us  [the longest x1 24.8 us: layer(): other_a = lax.ppermute(own[:half], 'dp', perm=[(0, 1), (1, 0)])]
    ppermute x1 -> x2, starting transfers between devices: 6.42 us -> 6.52 us  [the longest x1 6.42 us: layer(): other_a = lax.ppermute(own[:half], 'dp', perm=[(0, 1), (1, 0)])]
  transfers between devices with their start and end apart: 3 -> 4, of which waited for: 2 -> 3; matrix products, arithmetic and copies ran while one was open for 4% -> 4% of each run, Pallas kernels for 0% -> 0%
where the time goes in v5:
time: 123 us
  waiting for transfers between devices  71.8 us (58%)
  starting transfers between devices  29.2 us (24%)
  local copies, waits for them, and re-layouts  11.3 us (9%)
  matrix products  6.9 us (6%)
  other arithmetic  3.03 us (2%)
    all_to_all x1, waiting for transfers between devices, layer(): lax.all_to_all(first, ('seq', 'dp'), split_axis=0, concat_axis=0, tiled=T...  30 us
    ppermute x1, waiting for transfers between devices, layer(): other_a = lax.ppermute(own[:half], 'dp', perm=[(0, 1), (1, 0)])  24.8 us
    ppermute x1, waiting for transfers between devices, layer(): other_b = lax.ppermute(own[half:], 'dp', perm=[(0, 1), (1, 0)])  16.9 us
    all_to_all x1, starting transfers between devices, layer(): lax.all_to_all(first, ('seq', 'dp'), split_axis=0, concat_axis=0, tiled=T...  15.6 us
    all_to_all x1, starting transfers between devices, layer(): lax.all_to_all(unmixed, ('dp', 'seq'), split_axis=0, concat_axis=0, tiled...  7 us
    ppermute x1, starting transfers between devices, layer(): other_a = lax.ppermute(own[:half], 'dp', perm=[(0, 1), (1, 0)])  6.42 us
    unnamed x16, local copies, waits for them, and re-layouts  2.82 us
  transfers between devices with their start and end apart: 4, of which 3 were waited for; matrix products, arithmetic and copies ran while one was open for 4% of the time, Pallas kernels for 0%

profile of v5, /device:TPU:1, one launch (start us, length us, event | category | flops | bytes accessed | tf_op | source)
XLA Modules:
  0.0 123.0 jit_solution(4289157288204959382)
XLA Ops:
  0.6 0.0 copy-start
  0.6 1.4 %fusion.3 = bf16[2,256,512]{2,1,0:T(8,128)(2,1)S(1)} fusion(bf16[1,2,256,512]{3,2,1,0:T(8,128)(2,1)} %param.7, bf16[1,2,256,512]{3,2,1,0:T(8,128)(2,1)} %param.11), kind=kLoop, calls=%fused_computation.11 | loop fusion | flops 1048576 | bytes 1572864 | tf_op jit(solution)/shard_map/convert_element_type | solution.py:20
  2.0 1.7 %fusion = bf16[256,2,1024]{0,2,1:T(8,128)(2,1)S(1)} fusion(bf16[2,256,256]{2,1,0:T(8,128)(2,1)} %param.9, bf16[2,256,512]{2,1,0:T(8,128)(2,1)S(1)} %fusion.3, bf16[2,256,512]{2,1,0:T(8,128)(2,1)} %bitcast.52), kind=kOutput, calls=%fused_computation.5 | convolution fusion | flops 271056896 | bytes 2359296 | tf_op jit(solution)/shard_map/rij,rjf->irf/dot_general | solution.py:28
  3.7 2.1 %copy.29 = bf16[256,2,1024]{2,1,0:T(2,128)(2,1)} copy(bf16[256,2,1024]{0,2,1:T(8,128)(2,1)S(1)} %fusion) | data formatting | bytes 2097152 | tf_op jit(solution)/shard_map/convert_element_type | solution.py:28
  5.8 15.6 %all-to-all-start = ((bf16[256,2,1024]{2,1,0:T(2,128)(2,1)}), bf16[256,2,1024]{2,1,0:T(2,128)(2,1)S(1)}, u32[]{:S(2)}, u32[]{:S(2)}) async-start(bf16[256,2,1024]{2,1,0:T(2,128)(2,1)} %copy.29), calls=%async_computation | async-start | bytes 2097152 | tf_op jit(solution)/shard_map/all_to_all | solution.py:29
  21.5 0.1 copy.30
  21.6 0.1 reshape.32
  21.7 0.1 copy.32
  21.8 0.5 constant_dynamic-slice_fusion
  22.4 0.1 maximum_convert_fusion
  22.6 1.3 %copy.34 = f32[256,1024]{0,1:T(8,128)} copy(f32[256,1024]{1,0:T(8,128)S(1)} %maximum_convert_fusion) | data formatting | bytes 2097152 | tf_op jit(solution)/shard_map/concatenate | solution.py:41
  23.9 30.0 %all-to-all-done = bf16[256,2,1024]{2,1,0:T(2,128)(2,1)S(1)} async-done(((bf16[256,2,1024]{2,1,0:T(2,128)(2,1)}), bf16[256,2,1024]{2,1,0:T(2,128)(2,1)S(1)}, u32[]{:S(2)}, u32[]{:S(2)}) %all-to-all-start) | async-done | bytes 1048608 | tf_op jit(solution)/shard_map/all_to_all | solution.py:29
  53.9 1.0 copy-done.1
  54.9 1.9 %convolution_bitcast_fusion.1 = f32[2,256,1024]{1,2,0:T(8,128)S(1)} fusion(bf16[128,2,2,1024]{3,2,1,0:T(2,128)(2,1)} %bitcast.47, bf16[256,128,2]{1,0,2:T(8,128)(2,1)S(1)} %copy.32), kind=kOutput, calls=%fused_computation.2 | convolution fusion | flops 268435456 | bytes 3276800 | tf_op jit(solution)/shard_map/qkl,kslf->sqf/dot_general | solution.py:31
  56.8 1.5 %fusion.1 = bf16[2,256,1024]{2,1,0:T(8,128)(2,1)} fusion(f32[2,256,1024]{1,2,0:T(8,128)S(1)} %convolution_bitcast_fusion.1, f32[256,1024]{0,1:T(8,128)S(1)} %copy-done.2, bf16[1,256,256]{2,1,0:T(8,128)(2,1)S(1)} %constant_dynamic-slice_fusion.1), kind=kOutput, calls=%fused_computation.6 | convolution fusion | flops 270008320 | bytes 4325376 | tf_op jit(solution)/shard_map/qr,sqf->srf/dot_general | solution.py:43
  58.3 2.3 %reshape.33 = bf16[256,2,1024]{2,1,0:T(2,128)(2,1)} reshape(bf16[2,256,1024]{2,1,0:T(8,128)(2,1)} %fusion.1) | data formatting | bytes 2097152 | tf_op jit(solution)/shard_map/reshape | solution.py:44
  60.6 7.0 %all-to-all-start.1 = ((bf16[256,2,1024]{2,1,0:T(2,128)(2,1)}), bf16[256,2,1024]{2,1,0:T(2,128)(2,1)}, u32[]{:S(2)}, u32[]{:S(2)}) async-start(bf16[256,2,1024]{2,1,0:T(2,128)(2,1)} %reshape.33), calls=%async_computation.1 | async-start | bytes 2097152 | tf_op jit(solution)/shard_map/all_to_all | solution.py:45
  67.6 0.1 fusion.5
  67.8 6.4 %collective-permute-start = (f32[128,512]{0,1:T(8,128)S(1)}, f32[128,512]{0,1:T(8,128)S(1)}, u32[]{:S(2)}, u32[]{:S(2)}) collective-permute-start(f32[128,512]{0,1:T(8,128)S(1)} %get-tuple-element.14), channel_id=1, source_target_pairs={{0,1},{1,0},{2,3},{3,2},{4,5},{5,4},{6,7},{7,6},{8,9},{9,8},{10,11... | collective-permute-start | bytes 786440 | tf_op jit(solution)/shard_map/ppermute | solution.py:38
  74.2 0.1 collective-permute-start.1
  74.3 0.1 reshape.34
  74.4 0.3 copy.37
  74.7 0.2 reshape.35
  74.9 0.2 copy.39
  75.1 24.8 %collective-permute-done = f32[128,512]{0,1:T(8,128)S(1)} collective-permute-done((f32[128,512]{0,1:T(8,128)S(1)}, f32[128,512]{0,1:T(8,128)S(1)}, u32[]{:S(2)}, u32[]{:S(2)}) %collective-permute-start) | collective-permute-done | bytes 262176 | tf_op jit(solution)/shard_map/ppermute | solution.py:38
  100.0 16.9 %collective-permute-done.1 = f32[128,512]{0,1:T(8,128)S(1)} collective-permute-done((f32[128,512]{0,1:T(8,128)S(1)}, f32[128,512]{0,1:T(8,128)S(1)}, u32[]{:S(2)}, u32[]{:S(2)}) %collective-permute-start.1) | collective-permute-done | bytes 262176 | tf_op jit(solution)/shard_map/ppermute | solution.py:39
  116.9 0.2 copy.40
  117.1 0.1 maximum_select_fusion
  117.2 1.8 %copy.41 = f32[256,2,512]{2,1,0:T(2,128)} copy(f32[256,2,512]{2,0,1:T(8,128)S(1)} %maximum_select_fusion) | data formatting | bytes 2097152
  119.0 1.8 %convolution_bitcast_fusion = f32[2,256,1024]{2,1,0:T(8,128)S(1)} fusion(bf16[2,256,256]{1,2,0:T(8,128)(2,1)S(1)} %reshape.35, bf16[256,2,1024]{2,1,0:T(2,128)(2,1)} %all-to-all-done.1), kind=kOutput, calls=%fused_computation.1 | convolution fusion | flops 268435456 | bytes 3407872 | tf_op jit(solution)/shard_map/rij,irf->rjf/dot_general | solution.py:46
  120.8 0.9 fusion.12
  121.7 1.3 %fusion.14 = (bf16[1,2,256,512]{3,2,1,0:T(8,128)(2,1)}, bf16[1,2,256,512]{3,2,1,0:T(8,128)(2,1)}) fusion(f32[2,256,1024]{2,1,0:T(8,128)S(1)} %convolution_bitcast_fusion, bf16[1,2,256,512]{3,2,1,0:T(8,128)(2,1)S(1)} %copy-done.4, bf16[1,2,256,512]{3,2,1,0:T(8,128)(2,1)S(1)} %copy-done.3), kind=kLoop, calls=%fused_computation.25 | loop fusion | flops 1572864 | bytes 3145728 | tf_op jit(solution)/shard_map/broadcast_in_dim | solution.py:50
  (17 shorter events, 0.2 us)
Async XLA Ops:
  0.6 21.2 %copy-start = (bf16[256,2,512]{2,1,0:T(2,128)(2,1)S(1)}, bf16[256,2,512]{2,1,0:T(2,128)(2,1)}, u32[]{:S(2)}) copy-start(bf16[256,2,512]{2,1,0:T(2,128)(2,1)} %param.8) | copy-start | bytes 1572868
  3.7 17.8 %copy-start.6 = (bf16[2,256,256]{2,1,0:T(8,128)(2,1)S(1)}, bf16[2,256,256]{2,1,0:T(8,128)(2,1)}, u32[]{:S(2)}) copy-start(bf16[2,256,256]{2,1,0:T(8,128)(2,1)} %param.10) | copy-start | bytes 786436
  5.8 48.1 %all-to-all-start = ((bf16[256,2,1024]{2,1,0:T(2,128)(2,1)}), bf16[256,2,1024]{2,1,0:T(2,128)(2,1)S(1)}, u32[]{:S(2)}, u32[]{:S(2)}) async-start(bf16[256,2,1024]{2,1,0:T(2,128)(2,1)} %copy.29), calls=%async_computation | async-start | bytes 2097152 | tf_op jit(solution)/shard_map/all_to_all | solution.py:29
  53.9 1.0 copy-start.1
  54.9 1.9 %copy-start.2 = (f32[256,1024]{0,1:T(8,128)S(1)}, f32[256,1024]{0,1:T(8,128)}, u32[]{:S(2)}) copy-start(f32[256,1024]{0,1:T(8,128)} %copy.34) | copy-start | bytes 3145732
  60.6 58.4 %all-to-all-start.1 = ((bf16[256,2,1024]{2,1,0:T(2,128)(2,1)}), bf16[256,2,1024]{2,1,0:T(2,128)(2,1)}, u32[]{:S(2)}, u32[]{:S(2)}) async-start(bf16[256,2,1024]{2,1,0:T(2,128)(2,1)} %reshape.33), calls=%async_computation.1 | async-start | bytes 2097152 | tf_op jit(solution)/shard_map/all_to_all | solution.py:45
  67.6 6.7 %copy-start.5 = (bf16[2,256,256]{2,1,0:T(8,128)(2,1)S(1)}, bf16[2,256,256]{2,1,0:T(8,128)(2,1)}, u32[]{:S(2)}) copy-start(bf16[2,256,256]{2,1,0:T(8,128)(2,1)} %param.9) | copy-start | bytes 786436
  67.8 32.2 %collective-permute-start = (f32[128,512]{0,1:T(8,128)S(1)}, f32[128,512]{0,1:T(8,128)S(1)}, u32[]{:S(2)}, u32[]{:S(2)}) collective-permute-start(f32[128,512]{0,1:T(8,128)S(1)} %get-tuple-element.14), channel_id=1, source_target_pairs={{0,1},{1,0},{2,3},{3,2},{4,5},{5,4},{6,7},{7,6},{8,9},{9,8},{10,11... | collective-permute-start | bytes 786440 | tf_op jit(solution)/shard_map/ppermute | solution.py:38
  74.2 42.6 %collective-permute-start.1 = (f32[128,512]{0,1:T(8,128)S(1)}, f32[128,512]{0,1:T(8,128)S(1)}, u32[]{:S(2)}, u32[]{:S(2)}) collective-permute-start(f32[128,512]{0,1:T(8,128)S(1)} %get-tuple-element.15), channel_id=1, source_target_pairs={{0,1},{1,0},{2,3},{3,2},{4,5},{5,4},{6,7},{7,6},{8,9},{9,8},{10,11... | collective-permute-start | bytes 786440 | tf_op jit(solution)/shard_map/ppermute | solution.py:39
  119.0 2.7 %copy-start.3 = (bf16[1,2,256,512]{3,2,1,0:T(8,128)(2,1)S(1)}, bf16[1,2,256,512]{3,2,1,0:T(8,128)(2,1)}, u32[]{:S(2)}) copy-start(bf16[1,2,256,512]{3,2,1,0:T(8,128)(2,1)} %param.7) | copy-start | bytes 1572868
  119.0 2.7 %copy-start.4 = (bf16[1,2,256,512]{3,2,1,0:T(8,128)(2,1)S(1)}, bf16[1,2,256,512]{3,2,1,0:T(8,128)(2,1)}, u32[]{:S(2)}) copy-start(bf16[1,2,256,512]{3,2,1,0:T(8,128)(2,1)} %param.11) | copy-start | bytes 1572868
